TPU v7x, 32 devices: a whole 2x2x4 slice. The times are simulated.
32 devices in a mesh: req: 2 (over x), seq: 16 (over z, y, core).
Axes of the slice: x: 2, y: 2, z: 4, core: 2. Of those that a mesh axis runs over, the one named last changes fastest.
Arguments:
- states: bfloat16 [4, 4, 4544], P(None, 'req', 'seq'), may hold values from -6 to 6
- kv_cache: bfloat16 [4, 8192, 128], P('req', 'seq'), may hold values from -48 to 48, as said below
- lengths: int32 [4], replicated, may hold values from 1 to 8188, as said below
- placement: int32 [4], replicated, may hold values from 0 to 3, each once
- norm_gain: bfloat16 [4544], replicated, may hold values from 0.25 to 1.75
- norm_bias: bfloat16 [4544], replicated, may hold values from -1.5 to 1.5
- w_query: bfloat16 [4544, 4544], P('req', 'seq'), may hold values from -0.09375 to 0.09375
- w_keyval: bfloat16 [4544, 128], P('req'), may hold values from -0.09375 to 0.09375
- w_out: bfloat16 [4544, 4544], P('seq', 'req'), may hold values from -0.09375 to 0.09375
- w_up: bfloat16 [4544, 18176], P('req', 'seq'), may hold values from -0.09375 to 0.09375
- w_down: bfloat16 [18176, 4544], P('seq', 'req'), may hold values from -0.046875 to 0.046875
Outputs:
- new_states: bfloat16 [4, 4, 4544], P(None, 'req', 'seq')
- new_cache: bfloat16 [4, 8192, 128], P('req', 'seq')
Inputs may be any that keep to these rules, and one draw needn't show every extreme that they name: Request r's cache holds its first lengths[r] positions; some request has exactly 8188. `kv_cache`: row i is the cache of request placement[i]; positions at or beyond that request's length hold arbitrary values. `placement`: each request is served by exactly one slot.
All inputs are finite; a program needn't handle non-finite values.
Results may differ from a plain program's by a relative error of at most 0.012.
The roundings to bfloat16 on the way count: a program that leaves them out, or rounds other values in their place, can miss the bound.
Values may be sent and summed in bfloat16 or wider, within the bound.
No kernel may reach another device: no remote copies, remote signals or barrier semaphores. Data moves between devices by JAX's collectives and lax.ppermute only.
A program may use at most 192 MiB of HBM per device.

v0:
```python
import jax
import jax.numpy as jnp
from jax import lax
from jax.sharding import PartitionSpec as P

EPSILON = 1e-05
NEGATIVE = -1e30
ALL = ("req", "seq")


def layer_norm(row_block, norm_gain, norm_bias):
    values = row_block.astype(jnp.float32)
    average = jnp.mean(values, axis=-1, keepdims=True)
    centered = values - average
    spread = jnp.mean(centered * centered, axis=-1, keepdims=True)
    scaled = centered * lax.rsqrt(spread + EPSILON)
    return (scaled * norm_gain.astype(jnp.float32) + norm_bias.astype(jnp.float32)).astype(
        jnp.bfloat16
    )


def rotate(vectors, positions):
    head_width = vectors.shape[-1]
    half_width = head_width // 2
    frequency = 10000.0 ** (-(jnp.arange(half_width, dtype=jnp.float32) * 2.0) / head_width)
    angles = positions.astype(jnp.float32)[:, None] * frequency[None, :]
    cosine = jnp.concatenate([jnp.cos(angles), jnp.cos(angles)], axis=-1)[:, None, :]
    sine_wave = jnp.concatenate([jnp.sin(angles), jnp.sin(angles)], axis=-1)[:, None, :]
    turned = jnp.concatenate([-vectors[..., half_width:], vectors[..., :half_width]], axis=-1)
    return vectors * cosine + turned * sine_wave


def shards(
    states,
    kv_cache,
    lengths,
    placement,
    norm_gain,
    norm_bias,
    w_query,
    w_keyval,
    w_out,
    w_up,
    w_down,
):
    steps = states.shape[0]
    group_rows = kv_cache.shape[0]
    seg_length = kv_cache.shape[1]
    head_width = kv_cache.shape[2] // 2
    model_width = norm_gain.shape[0]
    head_count = model_width // head_width
    slice_width = states.shape[2]
    part_width = w_query.shape[0]
    total = placement.shape[0]
    req_size = total // group_rows
    seq_size = model_width // slice_width
    rows = steps * total
    group_index = lax.axis_index("req")
    shard_index = lax.axis_index("seq")
    own_requests = lax.dynamic_slice_in_dim(placement, group_index * group_rows, group_rows, 0)
    slot_lengths = jnp.take(lengths, own_requests)
    step_offsets = jnp.arange(steps, dtype=jnp.int32)
    positions = slot_lengths[None, :] + step_offsets[:, None]
    every = lax.all_gather(states, ALL, axis=0, tiled=False)
    every = every.reshape(req_size, seq_size, steps, group_rows, slice_width)
    every = every.transpose(2, 0, 3, 1, 4).reshape(steps, total, model_width)
    current_all = jnp.take(every, placement, axis=1)
    normed = layer_norm(current_all.reshape(rows, model_width), norm_gain, norm_bias)
    normed_part = lax.dynamic_slice_in_dim(normed, group_index * part_width, part_width, 1)
    part_query = jnp.dot(normed_part, w_query, preferred_element_type=jnp.float32)
    part_keyval = jnp.dot(normed_part, w_keyval, preferred_element_type=jnp.float32)
    part_up = jnp.dot(normed_part, w_up, preferred_element_type=jnp.float32)
    first = lax.psum(jnp.concatenate([part_query, part_keyval, part_up], axis=1), "req")
    query_raw = first[:, :slice_width].astype(jnp.bfloat16).reshape(steps, total, slice_width)
    keyval = first[:, slice_width : slice_width + 2 * head_width].reshape(
        steps, total, 2 * head_width
    )
    up_part = first[:, slice_width + 2 * head_width :]
    own_query = lax.dynamic_slice_in_dim(query_raw, group_index * group_rows, group_rows, 1)
    query_all = lax.all_gather(own_query, "seq", axis=2, tiled=True)
    flat_positions = positions.reshape(-1)
    query_rows = rotate(
        query_all.astype(jnp.float32).reshape(steps * group_rows, head_count, head_width),
        flat_positions,
    ).astype(jnp.bfloat16)
    own_keyval = lax.dynamic_slice_in_dim(keyval, group_index * group_rows, group_rows, 1)
    own_keyval = own_keyval.reshape(steps * group_rows, 2 * head_width)
    new_key = rotate(own_keyval[:, None, :head_width], flat_positions)[:, 0, :]
    new_entry = jnp.concatenate([new_key, own_keyval[:, head_width:]], axis=-1).astype(jnp.bfloat16)
    new_entry = new_entry.reshape(steps, group_rows, 2 * head_width)
    local_slots = jnp.arange(seg_length, dtype=jnp.int32)
    global_positions = shard_index * seg_length + local_slots
    cache_now = kv_cache
    for step_index in range(steps):
        write_mask = global_positions[None, :] == positions[step_index][:, None]
        cache_now = jnp.where(write_mask[:, :, None], new_entry[step_index][:, None, :], cache_now)
    key_rows = cache_now[:, :, :head_width]
    value_rows = cache_now[:, :, head_width:]
    query_heads = (
        query_rows.reshape(steps, group_rows, head_count, head_width)
        .transpose(1, 0, 2, 3)
        .reshape(group_rows, steps * head_count, head_width)
    )
    scores = jnp.einsum(
        "gqd,gsd->gqs", query_heads, key_rows, preferred_element_type=jnp.float32
    ) * head_width ** (-0.5)
    valid = global_positions[None, None, :] <= positions.T[:, :, None]
    valid = jnp.broadcast_to(
        valid[:, :, None, :], (group_rows, steps, head_count, seg_length)
    ).reshape(group_rows, steps * head_count, seg_length)
    local_peak = jnp.max(jnp.where(valid, scores, NEGATIVE), axis=-1)
    weights = jnp.where(valid, jnp.exp(scores - local_peak[:, :, None]), 0.0)
    local_total = jnp.sum(weights, axis=-1)
    local_weighted = jnp.einsum(
        "gqs,gsd->gqd", weights, value_rows, preferred_element_type=jnp.float32
    )
    peak_buffer = jnp.full((total, steps * head_count), NEGATIVE, jnp.float32)
    peak_buffer = lax.dynamic_update_slice_in_dim(
        peak_buffer, local_peak, group_index * group_rows, 0
    )
    peak = lax.pmax(peak_buffer, ALL)
    own_peak = lax.dynamic_slice_in_dim(peak, group_index * group_rows, group_rows, 0)
    scale = jnp.exp(local_peak - own_peak)
    packed = jnp.concatenate(
        [local_weighted * scale[:, :, None], (local_total * scale)[:, :, None]], axis=-1
    )
    packed_buffer = jnp.zeros((total, steps * head_count, head_width + 1), jnp.float32)
    packed_buffer = lax.dynamic_update_slice_in_dim(
        packed_buffer, packed, group_index * group_rows, 0
    )
    summed = lax.psum(packed_buffer, ALL)
    mixed = summed[:, :, :head_width] / summed[:, :, head_width:]
    mixed = (
        mixed.reshape(total, steps, model_width)
        .transpose(1, 0, 2)
        .reshape(rows, model_width)
        .astype(jnp.bfloat16)
    )
    mixed_part = lax.dynamic_slice_in_dim(mixed, shard_index * slice_width, slice_width, 1)
    hidden = jax.nn.gelu(up_part, approximate=False).astype(jnp.bfloat16)
    partial_sum = jnp.dot(mixed_part, w_out, preferred_element_type=jnp.float32) + jnp.dot(
        hidden, w_down, preferred_element_type=jnp.float32
    )
    out_buffer = jnp.zeros((rows, model_width), jnp.float32)
    out_buffer = lax.dynamic_update_slice_in_dim(
        out_buffer, partial_sum, group_index * part_width, 1
    )
    branch = lax.psum(out_buffer, ALL).reshape(steps, total, model_width)
    inverse = jnp.zeros((total,), jnp.int32).at[placement].set(jnp.arange(total, dtype=jnp.int32))
    own_inverse = lax.dynamic_slice_in_dim(inverse, group_index * group_rows, group_rows, 0)
    own_branch = jnp.take(branch, own_inverse, axis=1)
    own_branch = lax.dynamic_slice_in_dim(own_branch, shard_index * slice_width, slice_width, 2)
    new_states = (states.astype(jnp.float32) + own_branch).astype(jnp.bfloat16)
    return (new_states, cache_now)


def solution(mesh):
    in_specs = (
        P(None, "req", "seq"),
        P("req", "seq", None),
        P(),
        P(),
        P(),
        P(),
        P("req", "seq"),
        P("req", None),
        P("seq", "req"),
        P("req", "seq"),
        P("seq", "req"),
    )
    out_specs = (P(None, "req", "seq"), P("req", "seq", None))
    return jax.shard_map(shards, mesh=mesh, in_specs=in_specs, out_specs=out_specs, check_vma=False)
```

profile of v0, /device:TPU:8, one launch (start us, length us, event | category | flops | bytes accessed | tf_op | source)
XLA Modules:
  0.0 437.4 jit_solution(13402356280962080718)
XLA Ops:
  7.2 0.8 compare_select_fusion.2
  8.0 0.7 compare_and_fusion
  8.6 0.8 dynamic-slice.1
  9.4 0.8 dynamic-slice.2
  10.2 38.8 %all-gather = bf16[128,2,284]{2,1,0:T(2,128)(2,1)S(1)} all-gather(bf16[4,2,284]{2,1,0:T(2,128)(2,1)} %param.11), channel_id=2, replica_groups=mesh['req'=2,'seq'=16] {'req','seq'}, dimensions={0}, use_global_device_ids=true | all-gather | bytes 149952 | tf_op jit(solution)/shard_map/all_gather | solution.py:64
  49.0 0.3 reshape.348
  49.4 0.7 gather_fusion.1
  50.1 0.3 convert_reduce_fusion
  50.4 0.3 fusion.5
  51.3 3.5 fusion.96
  54.8 0.3 fusion.94
  55.1 0.4 fusion.95
  55.5 0.8 concatenate.40
  56.5 0.6 gather_fusion
  57.7 0.1 copy.81
  58.0 0.2 reshape.346
  58.3 19.3 %all-reduce.4.cloned.1.call-done = f32[16,1548]{1,0:T(8,128)} async-done(((f32[16,1548]{1,0:T(8,128)}), f32[16,1548]{1,0:T(8,128)}) %all-reduce.4.cloned.1.call-update) | async-done | bytes 99088 | tf_op jit(solution)/shard_map/psum | solution.py:73
  77.6 0.8 slice.99
  78.4 0.7 slice.124
  79.2 0.2 copy.88
  79.4 32.2 %all_gather.11 = bf16[4,2,4544]{0,1,2:T(2,128)(2,1)} all-gather(bf16[4,2,284]{0,1,2:T(2,128)(2,1)S(1)} %copy.88), channel_id=1, replica_groups=mesh['req'=2,'seq'=16] {'seq'}, dimensions={2}, use_global_device_ids=true | all-gather | bytes 77248 | tf_op jit(solution)/shard_map/all_gather | solution.py:80
  111.6 5.2 %copy.73 = bf16[4,2,4544]{2,0,1:T(4,128)(2,1)S(1)} copy(bf16[4,2,4544]{0,1,2:T(2,128)(2,1)} %all_gather.11) | data formatting | bytes 145408 | tf_op jit(solution)/shard_map/all_gather | solution.py:80
  116.8 0.2 reshape.351
  117.1 0.2 reshape.350
  117.9 0.2 copy.78
  118.1 0.2 fusion.8
  118.2 0.2 copy.80
  118.5 0.2 select_select_fusion
  118.8 0.5 select_reduce_fusion
  119.3 41.3 %pmax.7 = f32[4,284]{1,0:T(4,128)S(1)} all-reduce(f32[4,284]{1,0:T(4,128)S(1)} %constant_dynamic-update-slice_fusion.1), channel_id=1, replica_groups=mesh['req'=2,'seq'=16] {'req','seq'}, use_global_device_ids=true, to_apply=%region_5.6 | all-reduce | flops 1136 | bytes 9088 | tf_op jit(solution)/shard_map/pmax | solution.py:121
  160.6 0.4 fusion
  161.0 0.4 convolution_multiply_fusion.1
  161.5 0.2 copy.82
  161.7 0.8 copy-done.2
  162.6 0.6 scatter_custom_fusion
  163.2 129.3 %all-reduce.6.cloned.1.call-done = f32[4,284,65]{2,1,0:T(8,128)} async-done(((f32[4,284,65]{2,1,0:T(8,128)}), f32[4,284,65]{2,1,0:T(8,128)}) %all-reduce.6.cloned.1.call-update) | async-done | bytes 295376 | tf_op jit(solution)/shard_map/psum | solution.py:131
  292.5 1.5 slice_reduce_fusion
  294.0 1.3 fusion.1
  295.3 0.2 convert_element_type.69
  295.6 0.4 fusion.55
  296.0 0.2 copy-done.6
  296.2 3.4 convolution_add_fusion
  299.7 1.3 dynamic_update_slice.11
  301.1 0.8 copy.84
  302.0 0.8 copy.86
  302.9 125.7 %all-reduce.8.cloned.1.call-done = f32[4,4,4544]{2,0,1:T(4,128)} async-done(((f32[4,4,4544]{2,0,1:T(4,128)}), f32[4,4,4544]{2,0,1:T(4,128)}) %all-reduce.8.cloned.1.call-update) | async-done | bytes 290832 | tf_op jit(solution)/shard_map/psum | solution.py:148
  428.5 1.6 gather_fusion.2
  430.2 0.6 copy.85
  (81 shorter events, 3.2 us)
Async XLA Ops:
  7.2 288.4 %copy-start = (bf16[284,2272]{1,0:T(8,128)(2,1)S(1)}, bf16[284,2272]{1,0:T(8,128)(2,1)}, u32[]{:S(2)}) copy-start(bf16[284,2272]{1,0:T(8,128)(2,1)} %param.19) | copy-start | bytes 3871492
  7.2 70.4 %all-reduce.4.cloned.1.call-start = ((), (), s32[]{:S(2)}) async-start(), calls=%async_computation | async-start | bytes 212992 | tf_op jit(solution)/shard_map/psum | solution.py:73
  51.3 3.5 copy-start.4
  51.3 3.8 copy-start.3
  54.8 1.6 copy-start.8
  54.8 1.7 copy-start.1
  55.1 2.6 copy-start.5
  56.3 236.2 %all-reduce.6.cloned.1.call-start = ((), (), s32[]{:S(2)}) async-start(), calls=%async_computation.1 | async-start | bytes 1179648 | tf_op jit(solution)/shard_map/psum | solution.py:131
  161.7 0.8 copy-start.2
  162.6 266.0 %all-reduce.8.cloned.1.call-start = ((), (), s32[]{:S(2)}) async-start(), calls=%async_computation.2 | async-start | bytes 589824 | tf_op jit(solution)/shard_map/psum | solution.py:148
  295.3 0.9 copy-start.6
  301.0 129.2 %copy-start.7 = (bf16[4,2,284]{2,1,0:T(2,128)(2,1)S(1)}, bf16[4,2,284]{2,1,0:T(2,128)(2,1)}, u32[]{:S(2)}) copy-start(bf16[4,2,284]{2,1,0:T(2,128)(2,1)} %param.11) | copy-start | bytes 13636
Sparse Core Ops, SparseCore 0:
  56.4 21.1 all-reduce.3
  162.7 129.7 all-reduce.5
  302.1 126.4 all-reduce.7
where the time goes:
time: 438 us; the launch traced here: 437 us
  waiting for transfers between devices  274 us (63%)
  blocking collectives  112 us (26%)
  local copies, waits for them, and re-layouts  22.3 us (5%)
  between operations  14.2 us (3%)
  matrix products  8.89 us (2%)
  other arithmetic  5.32 us (1%)
    psum x1, waiting for transfers between devices, shards(): summed = lax.psum(packed_buffer, ALL)  129 us
    psum x1, waiting for transfers between devices, shards(): branch = lax.psum(out_buffer, ALL).reshape(steps, total, model_width)  126 us
    pmax x1, blocking collectives, shards(): peak = lax.pmax(peak_buffer, ALL)  41.3 us
    all_gather x1, blocking collectives, shards(): every = lax.all_gather(states, ALL, axis=0, tiled=False)  38.8 us
    all_gather x1, blocking collectives, shards(): query_all = lax.all_gather(own_query, 'seq', axis=2, tiled=True)  32.2 us
    psum x1, waiting for transfers between devices, shards(): lax.psum(jnp.concatenate([part_query, part_keyval, part_up], axis=1), 'req')  19.3 us
  transfers between devices with their start and end apart: 3, of which 3 were waited for; matrix products, arithmetic and copies ran while one was open for 1% of the time, Pallas kernels for 0%

commit v1 on v0

--- a/solution.py
+++ b/solution.py
@@ -6,6 +6,12 @@
 EPSILON = 1e-05
 NEGATIVE = -1e30
 ALL = ("req", "seq")
+
+
+def gather_and_add(x, axis):
+    pieces = lax.all_gather(x, axis, axis=0, tiled=False)
+    acc = pieces.sum(axis=0)
+    return acc
 
 
 def layer_norm(row_block, norm_gain, norm_bias):
@@ -128,7 +134,7 @@
     packed_buffer = lax.dynamic_update_slice_in_dim(
         packed_buffer, packed, group_index * group_rows, 0
     )
-    summed = lax.psum(packed_buffer, ALL)
+    summed = gather_and_add(packed_buffer, ALL)
     mixed = summed[:, :, :head_width] / summed[:, :, head_width:]
     mixed = (
         mixed.reshape(total, steps, model_width)

time: 438 us -> 410 us (0.936)
  waiting for transfers between devices: 274 us -> 242 us
  other arithmetic: 5.32 us -> 10.8 us
    psum x1 -> x0, waiting for transfers between devices: 129 us -> none  [shards(): summed = lax.psum(packed_buffer, ALL)]
    all_gather x0 -> x1, waiting for transfers between devices: none -> 97.1 us  [gather_and_add(): pieces = lax.all_gather(x, axis, axis=0, tiled=False)]
    reduce_sum x0 -> x1, other arithmetic: none -> 6.72 us  [gather_and_add(): acc = pieces.sum(axis=0)]
where the time goes in v1:
time: 410 us; the launch traced here: 409 us
  waiting for transfers between devices  242 us (59%)
  blocking collectives  112 us (27%)
  local copies, waits for them, and re-layouts  21.2 us (5%)
  between operations  14.2 us (3%)
  other arithmetic  10.8 us (3%)
  matrix products  8.9 us (2%)
    psum x1, waiting for transfers between devices, shards(): branch = lax.psum(out_buffer, ALL).reshape(steps, total, model_width)  125 us
    all_gather x1, waiting for transfers between devices, gather_and_add(): pieces = lax.all_gather(x, axis, axis=0, tiled=False)  97.1 us
    pmax x1, blocking collectives, shards(): peak = lax.pmax(peak_buffer, ALL)  41.3 us
    all_gather x1, blocking collectives, shards(): every = lax.all_gather(states, ALL, axis=0, tiled=False)  38.8 us
    all_gather x1, blocking collectives, shards(): query_all = lax.all_gather(own_query, 'seq', axis=2, tiled=True)  32.2 us
    psum x1, waiting for transfers between devices, shards(): lax.psum(jnp.concatenate([part_query, part_keyval, part_up], axis=1), 'req')  19.3 us
  transfers between devices with their start and end apart: 3, of which 3 were waited for; matrix products, arithmetic and copies ran while one was open for 1% of the time, Pallas kernels for 0%

profile of v1, /device:TPU:8, one launch (start us, length us, event | category | flops | bytes accessed | tf_op | source)
XLA Modules:
  0.0 409.4 jit_solution(7489681770783762930)
XLA Ops:
  7.2 0.8 compare_select_fusion.2
  8.0 0.7 compare_and_fusion
  8.6 0.8 dynamic-slice.1
  9.4 0.8 dynamic-slice.2
  10.2 38.8 %all-gather = bf16[128,2,284]{2,1,0:T(2,128)(2,1)S(1)} all-gather(bf16[4,2,284]{2,1,0:T(2,128)(2,1)} %param.11), channel_id=2, replica_groups=mesh['req'=2,'seq'=16] {'req','seq'}, dimensions={0}, use_global_device_ids=true | all-gather | bytes 149952 | tf_op jit(solution)/shard_map/all_gather | solution.py:70
  49.0 0.3 reshape.350
  49.4 0.7 gather_fusion.1
  50.1 0.3 convert_reduce_fusion
  50.4 0.3 fusion.5
  51.3 3.5 fusion.96
  54.8 0.3 fusion.94
  55.1 0.4 fusion.95
  55.5 0.8 concatenate.40
  56.5 0.6 gather_fusion
  57.7 0.1 copy.81
  58.0 0.2 reshape.348
  58.3 19.3 %all-reduce.3.cloned.1.call-done = f32[16,1548]{1,0:T(8,128)} async-done(((f32[16,1548]{1,0:T(8,128)}), f32[16,1548]{1,0:T(8,128)}) %all-reduce.3.cloned.1.call-update) | async-done | bytes 99088 | tf_op jit(solution)/shard_map/psum | solution.py:79
  77.6 0.8 slice.99
  78.4 0.7 slice.121
  79.2 0.2 copy.92
  79.4 32.2 %all_gather.17 = bf16[4,2,4544]{0,1,2:T(2,128)(2,1)} all-gather(bf16[4,2,284]{0,1,2:T(2,128)(2,1)S(1)} %copy.92), channel_id=1, replica_groups=mesh['req'=2,'seq'=16] {'seq'}, dimensions={2}, use_global_device_ids=true | all-gather | bytes 77248 | tf_op jit(solution)/shard_map/all_gather | solution.py:86
  111.6 5.2 %copy.73 = bf16[4,2,4544]{2,0,1:T(4,128)(2,1)S(1)} copy(bf16[4,2,4544]{0,1,2:T(2,128)(2,1)} %all_gather.17) | data formatting | bytes 145408 | tf_op jit(solution)/shard_map/all_gather | solution.py:86
  116.8 0.2 reshape.353
  117.1 0.2 reshape.352
  117.9 0.2 copy.78
  118.1 0.2 fusion.8
  118.2 0.2 copy.80
  118.5 0.2 select_select_fusion
  118.8 0.5 select_reduce_fusion
  119.3 41.3 %pmax.7 = f32[4,284]{1,0:T(4,128)S(1)} all-reduce(f32[4,284]{1,0:T(4,128)S(1)} %constant_dynamic-update-slice_fusion), channel_id=1, replica_groups=mesh['req'=2,'seq'=16] {'req','seq'}, use_global_device_ids=true, to_apply=%region_5.6 | all-reduce | flops 1136 | bytes 9088 | tf_op jit(solution)/shard_map/pmax | solution.py:127
  160.6 0.4 fusion
  161.0 0.4 convolution_multiply_fusion.1
  161.5 0.2 copy_dynamic-update-slice_fusion
  161.7 0.8 copy-done.2
  162.6 0.8 scatter_custom_fusion
  163.4 97.1 %all-gather.3.cloned.1.call-done = f32[32,4,284,65]{2,1,3,0:T(4,128)} async-done(((f32[1,4,284,65]{2,1,3,0:T(4,128)}), f32[32,4,284,65]{2,1,3,0:T(4,128)}) %all-gather.3.cloned.1.call-update) | async-done | bytes 9451536 | tf_op jit(solution)/shard_map/all_gather | solution.py:12
  260.5 6.7 %reduce_sum.39 = f32[4,284,65]{1,0,2:T(4,128)S(1)} reduce(f32[32,4,284,65]{2,1,3,0:T(4,128)} %all-gather.3.cloned.1.call-done, f32[]{:T(128)} %constant.57.clone.1), dimensions={0}, to_apply=%region_7.8 | reduce | flops 2289040 | bytes 9746884 | tf_op jit(solution)/shard_map/reduce_sum | solution.py:13
  267.3 0.2 copy.84
  267.5 0.2 convert_element_type.69
  267.9 0.4 fusion.55
  268.2 0.2 copy-done.6
  268.4 3.4 convolution_add_fusion
  271.9 1.3 dynamic_update_slice.12
  273.3 0.8 copy.86
  274.3 0.8 copy.88
  275.1 125.5 %all-reduce.5.cloned.1.call-done = f32[4,4,4544]{2,0,1:T(4,128)} async-done(((f32[4,4,4544]{2,0,1:T(4,128)}), f32[4,4,4544]{2,0,1:T(4,128)}) %all-reduce.5.cloned.1.call-update) | async-done | bytes 290832 | tf_op jit(solution)/shard_map/psum | solution.py:154
  400.6 1.6 gather_fusion.2
  402.3 0.6 copy.87
  (83 shorter events, 3.3 us)
Async XLA Ops:
  7.2 260.7 %copy-start = (bf16[284,2272]{1,0:T(8,128)(2,1)S(1)}, bf16[284,2272]{1,0:T(8,128)(2,1)}, u32[]{:S(2)}) copy-start(bf16[284,2272]{1,0:T(8,128)(2,1)} %param.19) | copy-start | bytes 3871492
  7.2 70.4 %all-reduce.3.cloned.1.call-start = ((), (), s32[]{:S(2)}) async-start(), calls=%async_computation | async-start | bytes 212992 | tf_op jit(solution)/shard_map/psum | solution.py:79
  51.3 3.5 copy-start.4
  51.3 3.8 copy-start.3
  54.8 1.6 copy-start.8
  54.8 1.7 copy-start.1
  55.1 2.6 copy-start.5
  56.3 204.2 %all-gather.3.cloned.1.call-start = ((), (), s32[]{:S(2)}) async-start(), calls=%async_computation.1 | async-start | bytes 13178880 | tf_op jit(solution)/shard_map/all_gather | solution.py:12
  161.7 0.8 copy-start.2
  162.5 238.1 %all-reduce.5.cloned.1.call-start = ((), (), s32[]{:S(2)}) async-start(), calls=%async_computation.2 | async-start | bytes 589824 | tf_op jit(solution)/shard_map/psum | solution.py:154
  267.5 0.9 copy-start.6
  273.2 129.0 %copy-start.7 = (bf16[4,2,284]{2,1,0:T(2,128)(2,1)S(1)}, bf16[4,2,284]{2,1,0:T(2,128)(2,1)}, u32[]{:S(2)}) copy-start(bf16[4,2,284]{2,1,0:T(2,128)(2,1)} %param.11) | copy-start | bytes 13636
Sparse Core Ops, SparseCore 0:
  56.4 21.1 all-reduce.2
  162.7 97.7 all-gather.2
  274.3 126.2 all-reduce.4
